TPU v7x, 256 devices: a whole 4x4x8 slice. The times are simulated.
256 devices in a mesh: row: 32 (over x, z_hi, y), col: 8 (over z_lo, core).
Axes of the slice: x: 4, y: 4, z: 8 (z_hi: 2, z_lo: 4; z = z_hi * 4 + z_lo), core: 2. Of those that a mesh axis runs over, the one named last changes fastest.
Arguments:
- tile_values: bfloat16 [32, 8, 256, 128, 128], P('row', 'col'), may hold values from -0.125 to 0.125
- tile_coords: int32 [32, 8, 2, 256], P('row', 'col'), may hold values from 0 to 63, as said below
- tile_counts: int32 [32, 8], P('row', 'col'), may hold values from 32 to 256, as said below
- features: bfloat16 [8, 32, 256, 256], P('col', 'row'), may hold values from -6 to 6
- weight_matrix: bfloat16 [256, 256], replicated, may hold values from -0.375 to 0.375
- out_grad: bfloat16 [32, 8, 256, 256], P('row', 'col'), may hold values from -6 to 6
Outputs:
- activated: bfloat16 [32, 8, 256, 256], P('row', 'col')
- feature_grad: float32 [8, 32, 256, 256], P('col', 'row')
- weight_grad: float32 [256, 256], replicated
Inputs may be any that keep to these rules, and one draw needn't show every extreme that they name: `tile_coords`: each device's 256 slots name distinct tile positions; the tile row is below 16. `tile_counts`: some device has all 256 slots live.
All inputs are finite; a program needn't handle non-finite values.
Results may differ from a plain program's by a relative error of at most 0.015.
Values may be sent and summed in bfloat16 or wider, within the bound.
No kernel may reach another device: no remote copies, remote signals or barrier semaphores. Data moves between devices by JAX's collectives and lax.ppermute only.
A program may use at most 128 MiB of HBM per device.

v0:
```python
import math
import jax
import jax.numpy as jnp
from jax import lax
from jax.sharding import PartitionSpec as P


def aggregate(values, pick_index, place_index, live_count, source, segments, transposed):
    slot_total = values.shape[0]
    block_size = math.gcd(slot_total, 32)
    tile_side = values.shape[1]
    width = source.shape[2]

    def block_step(block, totals):
        offset = block * block_size
        chosen = lax.dynamic_slice_in_dim(values, offset, block_size, 0)
        picks = lax.dynamic_slice_in_dim(pick_index, offset, block_size, 0)
        places = lax.dynamic_slice_in_dim(place_index, offset, block_size, 0)
        picked = source[picks]
        if transposed:
            products = jnp.einsum(
                "kij,kif->kjf", chosen, picked, preferred_element_type=jnp.float32
            )
        else:
            products = jnp.einsum(
                "kij,kjf->kif", chosen, picked, preferred_element_type=jnp.float32
            )
        is_live = offset + jnp.arange(block_size, dtype=jnp.int32) < live_count
        products = jnp.where(is_live[:, None, None], products, 0.0)
        return totals.at[places].add(products)

    start_totals = jnp.zeros((segments, tile_side, width), jnp.float32)
    upper = (live_count + block_size - 1) // block_size
    return lax.fori_loop(0, upper, block_step, start_totals)


def shards(tile_values, tile_coords, tile_counts, features, weight_matrix, out_grad):
    values = tile_values[0, 0]
    coords = tile_coords[0, 0]
    live_count = tile_counts[0, 0]
    tile_side = values.shape[1]
    sub_rows = features.shape[2]
    width = features.shape[3]
    n_col = lax.axis_size("col")
    row_tiles = n_col * sub_rows // tile_side
    column_block = lax.all_gather(features, "row", axis=1, tiled=True)
    col_source = column_block.reshape(-1, tile_side, width)
    col_tiles = col_source.shape[0]
    partial_value = aggregate(
        values, coords[1], coords[0], live_count, col_source, row_tiles, False
    )
    partial_value = partial_value.reshape(1, n_col, sub_rows, width)
    share = lax.psum_scatter(partial_value, "col", scatter_dimension=1, tiled=True)
    mixed = share.astype(jnp.bfloat16).reshape(sub_rows, width)
    pre = jnp.dot(mixed, weight_matrix, preferred_element_type=jnp.float32)
    sigma = jax.nn.sigmoid(pre)
    activated = (pre * sigma).astype(jnp.bfloat16)
    pre_grad = (
        out_grad.reshape(sub_rows, width).astype(jnp.float32) * sigma * (1.0 + pre * (1.0 - sigma))
    ).astype(jnp.bfloat16)
    weight_terms = jnp.dot(mixed.T, pre_grad, preferred_element_type=jnp.float32)
    own_grad = jnp.dot(pre_grad, weight_matrix.T, preferred_element_type=jnp.float32).astype(
        jnp.bfloat16
    )
    mixed_grad = lax.all_gather(own_grad.reshape(1, 1, sub_rows, width), "col", axis=1, tiled=True)
    row_source = mixed_grad.reshape(row_tiles, tile_side, width)
    back_partial = aggregate(values, coords[0], coords[1], live_count, row_source, col_tiles, True)
    back_partial = back_partial.reshape(1, -1, sub_rows, width)
    feature_grad = lax.psum_scatter(back_partial, "row", scatter_dimension=1, tiled=True)
    weight_grad = lax.psum(weight_terms, ("row", "col"))
    return (activated.reshape(1, 1, sub_rows, width), feature_grad, weight_grad)


def solution(mesh):
    return jax.shard_map(
        shards,
        mesh=mesh,
        in_specs=(
            P("row", "col", None, None, None),
            P("row", "col", None, None),
            P("row", "col"),
            P("col", "row", None, None),
            P(),
            P("row", "col", None, None),
        ),
        out_specs=(P("row", "col", None, None), P("col", "row", None, None), P()),
        check_vma=False,
    )
```

profile of v0, /device:TPU:32, one launch (start us, length us, event | category | flops | bytes accessed | tf_op | source)
XLA Modules:
  0.0 863.9 jit_solution(18019783541457873077)
XLA Ops:
  7.2 0.0 copy-start
  7.2 0.0 all-gather.4.cloned.1.call-start
  7.2 0.7 all-gather.4.cloned.1.call-update
  7.9 0.0 reduce-scatter.3.cloned.1.call-start
  8.6 0.8 fusion.13
  9.4 115.5 %all-gather.4.cloned.1.call-done = bf16[1,32,256,256]{3,2,0,1:T(8,128)(2,1)} async-done(((bf16[1,1,256,256]{3,2,0,1:T(8,128)(2,1)}), bf16[1,32,256,256]{3,2,0,1:T(8,128)(2,1)}) %all-gather.4.cloned.1.call-update) | async-done | bytes 4194320 | tf_op jit(solution)/shard_map/all_gather | solution.py:46
  124.9 0.2 broadcast_in_dim.40
  125.1 0.0 copy-start.4
  125.1 32.2 %while.20 = (s32[]{:T(128)}, f32[16,128,256]{2,1,0:T(8,128)S(1)}, s32[]{:T(128)}, s32[256]{0:T(256)S(1)}, s32[]{:T(128)}, /*index=5*/bf16[256,128,128]{2,1,0:T(8...) while((s32[]{:T(128)}, f32[16,128,256]{2,1,0:T(8,128)S(1)}, ...), condition=%wide.region_2.3_spmd, body=%wide.region_0.2_spmd.sunk | while | flops 270533888 | bytes 24122484 | solution.py:34
  125.1 0.7 add_compare_fusion.4
  125.8 0.1 compare_select_fusion.6
  125.9 4.2 gather_fusion
  130.1 4.6 convolution_select_fusion.4
  134.7 6.5 scatter_fusion
  141.2 0.7 add_compare_fusion.4
  141.9 0.1 compare_select_fusion.6
  142.0 4.2 gather_fusion
  146.2 4.6 convolution_select_fusion.4
  150.8 6.5 scatter_fusion
  157.3 0.0 copy-start.1
  157.3 1.3 copy-done.1
  158.6 0.0 reduce-scatter.3.cloned.1.call-update
  158.7 0.0 all-gather.6.cloned.1.call-start
  158.7 128.7 %reduce-scatter.3.cloned.1.call-done = f32[1,1,256,256]{3,2,1,0:T(8,128)} async-done(((f32[1,8,256,256]{3,2,1,0:T(8,128)}), f32[1,1,256,256]{3,2,1,0:T(8,128)}) %reduce-scatter.3.cloned.1.call-update) | async-done | bytes 262160 | tf_op jit(solution)/shard_map/reduce_scatter | solution.py:53
  287.4 0.0 copy-done
  287.4 0.0 copy-done.4
  287.5 1.9 fusion.5
  289.3 0.9 convolution_convert_fusion
  290.2 0.0 all-gather.6.cloned.1.call-update
  290.2 0.0 all-reduce.2.cloned.1.call-start
  290.3 0.0 copy-start.3
  290.3 12.0 %copy.11 = bf16[1,1,256,128,128]{3,4,2,1,0:T(8,128)(2,1)} copy(bf16[1,1,256,128,128]{4,3,2,1,0:T(8,128)(2,1)} %bitcast.38) | data formatting | bytes 16777216 | tf_op args[0]
  302.3 0.0 copy-done.3
  302.3 0.9 fusion.6
  303.3 0.0 all-reduce.2.cloned.1.call-update
  303.3 0.0 reduce-scatter.5.cloned.1.call-start
  303.3 23.7 %all-gather.6.cloned.1.call-done = bf16[2048,256]{1,0:T(8,128)(2,1)} async-done(((bf16[256,256]{1,0:T(8,128)(2,1)}), bf16[2048,256]{1,0:T(8,128)(2,1)}) %all-gather.6.cloned.1.call-update) | async-done | bytes 1048592 | tf_op jit(solution)/shard_map/all_gather | solution.py:65
  327.0 0.0 copy-start.2
  327.0 4.3 broadcast_in_dim.41
  331.3 0.0 copy-done.2
  331.3 30.8 %while.21 = (s32[]{:T(128)}, f32[64,128,256]{2,1,0:T(8,128)}, s32[]{:T(128)}, s32[256]{0:T(256)S(1)}, s32[]{:T(128)}, /*index=5*/bf16[256,128,128]{1,2,0:T(8,128...) while((s32[]{:T(128)}, f32[64,128,256]{2,1,0:T(8,128)}, ...), condition=%wide.region_6.7_spmd, body=%wide.region_4.6_spmd.sunk | while | flops 270533888 | bytes 24122484 | solution.py:34
  331.3 0.7 add_compare_fusion.5
  331.9 0.1 compare_select_fusion.7
  332.0 0.7 gather_fusion.1
  332.7 3.9 convolution_select_fusion.5
  336.6 10.0 %scatter_fusion.1 = f32[64,128,256]{2,1,0:T(8,128)} fusion(f32[64,128,256]{2,1,0:T(8,128)} %get-tuple-element.304, s32[32]{0:T(128)S(1)} %get-tuple-element.253, f32[32,128,256]{2,1,0:T(8,128)} %convolution_select_fusion.5), kind=kCustom, calls=%fused_computation.3.clone.1 | custom fusion | flops 1048576 | bytes 12583040 | tf_op jit(solution)/shard_map/while/body/scatter-add | solution.py:30
  346.6 0.7 add_compare_fusion.5
  347.2 0.1 compare_select_fusion.7
  347.3 0.7 gather_fusion.1
  348.0 3.9 convolution_select_fusion.5
  351.9 10.2 %scatter_fusion.1 = f32[64,128,256]{2,1,0:T(8,128)} fusion(f32[64,128,256]{2,1,0:T(8,128)} %get-tuple-element.304, s32[32]{0:T(128)S(1)} %get-tuple-element.253, f32[32,128,256]{2,1,0:T(8,128)} %convolution_select_fusion.5), kind=kCustom, calls=%fused_computation.3.clone.1 | custom fusion | flops 1048576 | bytes 12583040 | tf_op jit(solution)/shard_map/while/body/scatter-add | solution.py:30
  362.0 0.0 reduce-scatter.5.cloned.1.call-update
  362.1 224.9 %all-reduce.2.cloned.1.call-done = f32[256,256]{1,0:T(8,128)} async-done(((f32[256,256]{1,0:T(8,128)}), f32[256,256]{1,0:T(8,128)}) %all-reduce.2.cloned.1.call-update) | async-done | bytes 262160 | tf_op jit(solution)/shard_map/psum | solution.py:70
  586.9 268.8 %reduce-scatter.5.cloned.1.call-done = f32[1,1,256,256]{3,2,1,0:T(8,128)} async-done(((f32[1,32,256,256]{3,2,1,0:T(8,128)}), f32[1,1,256,256]{3,2,1,0:T(8,128)}) %reduce-scatter.5.cloned.1.call-update) | async-done | bytes 262160 | tf_op jit(solution)/shard_map/reduce_scatter | solution.py:69
  855.7 1.7 copy.31
  (4 shorter events, 0.0 us)
Async XLA Ops:
  7.2 280.3 %copy-start = (bf16[256,256]{1,0:T(8,128)(2,1)S(1)}, bf16[256,256]{1,0:T(8,128)(2,1)}, u32[]{:S(2)}) copy-start(bf16[256,256]{1,0:T(8,128)(2,1)} %param.14) | copy-start | bytes 393220
  7.2 117.7 %all-gather.4.cloned.1.call-start = ((), (), s32[]{:S(2)}) async-start(), calls=%async_computation.2 | async-start | bytes 4325376 | tf_op jit(solution)/shard_map/all_gather | solution.py:46
  7.9 279.5 %reduce-scatter.3.cloned.1.call-start = ((), (), s32[]{:S(2)}) async-start(), calls=%async_computation.3 | async-start | bytes 2359296 | tf_op jit(solution)/shard_map/reduce_scatter | solution.py:53
  125.1 162.4 %copy-start.4 = (bf16[1,1,256,256]{3,2,1,0:T(8,128)(2,1)S(1)}, bf16[1,1,256,256]{3,2,1,0:T(8,128)(2,1)}, u32[]{:S(2)}) copy-start(bf16[1,1,256,256]{3,2,1,0:T(8,128)(2,1)} %param.15) | copy-start | bytes 393220
  157.3 1.3 copy-start.1
  158.7 168.3 %all-gather.6.cloned.1.call-start = ((), (), s32[]{:S(2)}) async-start(), calls=%async_computation.6 | async-start | bytes 1179648 | tf_op jit(solution)/shard_map/all_gather | solution.py:65
  290.2 296.7 %all-reduce.2.cloned.1.call-start = ((), (), s32[]{:S(2)}) async-start(), calls=%async_computation.5 | async-start | bytes 524288 | tf_op jit(solution)/shard_map/psum | solution.py:70
  290.3 12.0 %copy-start.3 = (f32[1,1,256,256]{3,2,1,0:T(8,128)S(1)}, f32[1,1,256,256]{3,2,1,0:T(8,128)}, u32[]{:S(2)}) copy-start(f32[1,1,256,256]{3,2,1,0:T(8,128)} %reduce-scatter.3.cloned.1.call-done) | copy-start | bytes 786436
  303.3 552.5 %reduce-scatter.5.cloned.1.call-start = ((), (), s32[]{:S(2)}) async-start(), calls=%async_computation.4 | async-start | bytes 8650752 | tf_op jit(solution)/shard_map/reduce_scatter | solution.py:69
  327.0 4.3 copy-start.2
Sparse Core Ops, SparseCore 0:
  11.5 113.3 all-gather.3
  158.8 128.6 reduce-scatter.2
  290.4 36.5 all-gather.5
  332.9 254.0 all-reduce.1
  589.9 265.7 reduce-scatter.4
where the time goes:
time: 866 us; the launch traced here: 864 us
  waiting for transfers between devices  762 us (88%)
  other arithmetic  36.1 us (4%)
  local copies, waits for them, and re-layouts  30.1 us (3%)
  matrix products  20.6 us (2%)
  between operations  14.5 us (2%)
    reduce_scatter x1, waiting for transfers between devices, shards(): lax.psum_scatter(back_partial, 'row', scatter_dimension=1, tiled=True)  269 us
    psum x1, waiting for transfers between devices, shards(): weight_grad = lax.psum(weight_terms, ('row', 'col'))  225 us
    reduce_scatter x1, waiting for transfers between devices, shards(): lax.psum_scatter(partial_value, 'col', scatter_dimension=1, tiled=True)  129 us
    all_gather x1, waiting for transfers between devices, shards(): column_block = lax.all_gather(features, 'row', axis=1, tiled=True)  115 us
    scatter-add x4, other arithmetic, block_step(): return totals.at[places].add(products)  33.1 us
    all_gather x1, waiting for transfers between devices, shards(): lax.all_gather(own_grad.reshape(1, 1, sub_rows, width), 'col', axis=1, ti...  23.7 us
  transfers between devices with their start and end apart: 5, of which 5 were waited for; matrix products, arithmetic and copies ran while one was open for 6% of the time, Pallas kernels for 0%

commit v1 on v0

--- a/solution.py
+++ b/solution.py
@@ -67,7 +67,7 @@
     back_partial = aggregate(values, coords[0], coords[1], live_count, row_source, col_tiles, True)
     back_partial = back_partial.reshape(1, -1, sub_rows, width)
     feature_grad = lax.psum_scatter(back_partial, "row", scatter_dimension=1, tiled=True)
-    weight_grad = lax.psum(weight_terms, ("row", "col"))
+    weight_grad = jnp.sum(lax.all_gather(weight_terms, ("row", "col")), axis=0)
     return (activated.reshape(1, 1, sub_rows, width), feature_grad, weight_grad)
 
 

time: 866 us -> 1090 us (1.26)
  waiting for transfers between devices: 762 us -> 956 us
  other arithmetic: 36.1 us -> 58.3 us
    all_gather x0 -> x1, waiting for transfers between devices: none -> 452 us  [shards(): weight_grad = jnp.sum(lax.all_gather(weight_terms, ('row', 'col')), axis=0)]
    psum x1 -> x0, waiting for transfers between devices: 225 us -> none  [shards(): weight_grad = lax.psum(weight_terms, ('row', 'col'))]
    reduce_scatter x1, waiting for transfers between devices: 269 us -> 236 us  [shards(): lax.psum_scatter(back_partial, 'row', scatter_dimension=1, tiled=True)]
    reduce_sum x0 -> x1, other arithmetic: none -> 21.9 us  [shards(): weight_grad = jnp.sum(lax.all_gather(weight_terms, ('row', 'col')), axis=0)]
  transfers between devices with their start and end apart: 5 -> 5, of which waited for: 5 -> 5; matrix products, arithmetic and copies ran while one was open for 6% -> 7% of each run, Pallas kernels for 0% -> 0%
where the time goes in v1:
time: 1090 us; the launch traced here: 1080 us
  waiting for transfers between devices  956 us (88%)
  other arithmetic  58.3 us (5%)
  local copies, waits for them, and re-layouts  28.4 us (3%)
  matrix products  21.7 us (2%)
  between operations  14.5 us (1%)
    all_gather x1, waiting for transfers between devices, shards(): weight_grad = jnp.sum(lax.all_gather(weight_terms, ('row', 'col')), axis=0)  452 us
    reduce_scatter x1, waiting for transfers between devices, shards(): lax.psum_scatter(back_partial, 'row', scatter_dimension=1, tiled=True)  236 us
    reduce_scatter x1, waiting for transfers between devices, shards(): lax.psum_scatter(partial_value, 'col', scatter_dimension=1, tiled=True)  129 us
    all_gather x1, waiting for transfers between devices, shards(): column_block = lax.all_gather(features, 'row', axis=1, tiled=True)  115 us
    scatter-add x4, other arithmetic, block_step(): return totals.at[places].add(products)  33.5 us
    all_gather x1, waiting for transfers between devices, shards(): lax.all_gather(own_grad.reshape(1, 1, sub_rows, width), 'col', axis=1, ti...  22.7 us
    reduce_sum x1, other arithmetic, shards(): weight_grad = jnp.sum(lax.all_gather(weight_terms, ('row', 'col')), axis=0)  21.9 us
  transfers between devices with their start and end apart: 5, of which 5 were waited for; matrix products, arithmetic and copies ran while one was open for 7% of the time, Pallas kernels for 0%

profile of v1, /device:TPU:32, one launch (start us, length us, event | category | flops | bytes accessed | tf_op | source)
XLA Modules:
  0.0 1078.8 jit_solution(14926338428255874310)
XLA Ops:
  7.2 0.0 copy-start
  7.2 0.0 all-gather.6.cloned.1.call-start
  7.2 0.7 all-gather.6.cloned.1.call-update
  7.9 0.0 reduce-scatter.3.cloned.1.call-start
  8.6 0.8 fusion.13
  9.4 115.5 %all-gather.6.cloned.1.call-done = bf16[1,32,256,256]{3,2,0,1:T(8,128)(2,1)} async-done(((bf16[1,1,256,256]{3,2,0,1:T(8,128)(2,1)}), bf16[1,32,256,256]{3,2,0,1:T(8,128)(2,1)}) %all-gather.6.cloned.1.call-update) | async-done | bytes 4194320 | tf_op jit(solution)/shard_map/all_gather | solution.py:46
  124.9 0.2 broadcast_in_dim.40
  125.1 0.0 copy-start.3
  125.1 32.2 %while.20 = (s32[]{:T(128)}, f32[16,128,256]{2,1,0:T(8,128)S(1)}, s32[]{:T(128)}, s32[256]{0:T(256)S(1)}, s32[]{:T(128)}, /*index=5*/bf16[256,128,128]{2,1,0:T(8...) while((s32[]{:T(128)}, f32[16,128,256]{2,1,0:T(8,128)S(1)}, ...), condition=%wide.region_2.3_spmd, body=%wide.region_0.2_spmd.sunk | while | flops 270533888 | bytes 24122492 | solution.py:34
  125.1 0.1 compare_select_fusion.6
  125.2 4.2 gather_fusion
  129.4 0.7 add_compare_fusion.4
  130.1 4.6 convolution_select_fusion.4
  134.7 6.5 scatter_fusion
  141.2 0.1 compare_select_fusion.6
  141.3 4.2 gather_fusion
  145.5 0.7 add_compare_fusion.4
  146.2 4.6 convolution_select_fusion.4
  150.8 6.5 scatter_fusion
  157.3 0.0 copy-start.1
  157.3 1.3 copy-done.1
  158.6 0.0 reduce-scatter.3.cloned.1.call-update
  158.6 0.0 all-gather.8.cloned.1.call-start
  158.7 128.9 %reduce-scatter.3.cloned.1.call-done = f32[1,1,256,256]{3,2,1,0:T(8,128)} async-done(((f32[1,8,256,256]{3,2,1,0:T(8,128)}), f32[1,1,256,256]{3,2,1,0:T(8,128)}) %reduce-scatter.3.cloned.1.call-update) | async-done | bytes 262160 | tf_op jit(solution)/shard_map/reduce_scatter | solution.py:53
  287.6 0.0 copy-done
  287.6 0.0 copy-done.3
  287.6 1.9 fusion.5
  289.5 0.9 convolution_convert_fusion
  290.4 0.0 all-gather.8.cloned.1.call-update
  290.4 0.0 all-gather.10.cloned.1.call-start
  290.4 1.9 fusion.6
  292.3 0.0 all-gather.10.cloned.1.call-update
  292.3 0.0 reduce-scatter.5.cloned.1.call-start
  292.4 12.0 %copy.11 = bf16[1,1,256,128,128]{3,4,2,1,0:T(8,128)(2,1)} copy(bf16[1,1,256,128,128]{4,3,2,1,0:T(8,128)(2,1)} %bitcast.39) | data formatting | bytes 16777216 | tf_op args[0]
  304.4 22.7 %all-gather.8.cloned.1.call-done = bf16[2048,256]{1,0:T(8,128)(2,1)} async-done(((bf16[256,256]{1,0:T(8,128)(2,1)}), bf16[2048,256]{1,0:T(8,128)(2,1)}) %all-gather.8.cloned.1.call-update) | async-done | bytes 1048592 | tf_op jit(solution)/shard_map/all_gather | solution.py:65
  327.1 0.0 copy-start.2
  327.1 4.4 broadcast_in_dim.41
  331.4 0.0 copy-done.2
  331.4 31.2 %while.21 = (s32[]{:T(128)}, f32[64,128,256]{2,1,0:T(8,128)}, s32[]{:T(128)}, s32[256]{0:T(256)S(1)}, s32[]{:T(128)}, /*index=5*/bf16[256,128,128]{1,2,0:T(8,128...) while((s32[]{:T(128)}, f32[64,128,256]{2,1,0:T(8,128)}, ...), condition=%wide.region_6.7_spmd, body=%wide.region_4.6_spmd.sunk | while | flops 270533888 | bytes 24122492 | solution.py:34
  331.4 0.1 compare_select_fusion.7
  331.5 0.7 gather_fusion.1
  332.2 0.7 add_compare_fusion.5
  332.8 3.9 convolution_select_fusion.5
  336.8 10.2 scatter_fusion.1
  347.0 0.1 compare_select_fusion.7
  347.0 0.7 gather_fusion.1
  347.7 0.7 add_compare_fusion.5
  348.4 4.0 convolution_select_fusion.5
  352.4 10.3 scatter_fusion.1
  362.6 0.0 reduce-scatter.5.cloned.1.call-update
  362.6 451.9 %all-gather.10.cloned.1.call-done = f32[65536,256]{1,0:T(8,128)} async-done(((f32[256,256]{1,0:T(8,128)}), f32[65536,256]{1,0:T(8,128)}) %all-gather.10.cloned.1.call-update) | async-done | bytes 67108880 | tf_op jit(solution)/shard_map/all_gather | solution.py:70
  814.6 21.9 %reduce_sum.9 = f32[256,256]{1,0:T(8,128)} reduce(f32[256,256,256]{2,1,0:T(8,128)} %bitcast.13, f32[]{:T(128)} %constant.52.clone.1), dimensions={0}, to_apply=%region_8.9 | reduce | flops 16711680 | bytes 67371008 | tf_op jit(solution)/shard_map/reduce_sum | solution.py:70
  836.5 235.8 %reduce-scatter.5.cloned.1.call-done = f32[1,1,256,256]{3,2,1,0:T(8,128)} async-done(((f32[1,32,256,256]{3,2,1,0:T(8,128)}), f32[1,1,256,256]{3,2,1,0:T(8,128)}) %reduce-scatter.5.cloned.1.call-update) | async-done | bytes 262160 | tf_op jit(solution)/shard_map/reduce_scatter | solution.py:69
  (4 shorter events, 0.0 us)
Async XLA Ops:
  7.2 280.4 %copy-start = (bf16[256,256]{1,0:T(8,128)(2,1)S(1)}, bf16[256,256]{1,0:T(8,128)(2,1)}, u32[]{:S(2)}) copy-start(bf16[256,256]{1,0:T(8,128)(2,1)} %param.14) | copy-start | bytes 393220
  7.2 117.7 %all-gather.6.cloned.1.call-start = ((), (), s32[]{:S(2)}) async-start(), calls=%async_computation.2 | async-start | bytes 4325376 | tf_op jit(solution)/shard_map/all_gather | solution.py:46
  7.9 279.7 %reduce-scatter.3.cloned.1.call-start = ((), (), s32[]{:S(2)}) async-start(), calls=%async_computation.3 | async-start | bytes 2359296 | tf_op jit(solution)/shard_map/reduce_scatter | solution.py:53
  125.1 162.5 %copy-start.3 = (bf16[1,1,256,256]{3,2,1,0:T(8,128)(2,1)S(1)}, bf16[1,1,256,256]{3,2,1,0:T(8,128)(2,1)}, u32[]{:S(2)}) copy-start(bf16[1,1,256,256]{3,2,1,0:T(8,128)(2,1)} %param.15) | copy-start | bytes 393220
  157.3 1.3 copy-start.1
  158.6 168.4 %all-gather.8.cloned.1.call-start = ((), (), s32[]{:S(2)}) async-start(), calls=%async_computation.5 | async-start | bytes 1179648 | tf_op jit(solution)/shard_map/all_gather | solution.py:65
  290.4 524.2 %all-gather.10.cloned.1.call-start = ((), (), s32[]{:S(2)}) async-start(), calls=%async_computation.6 | async-start | bytes 67371008 | tf_op jit(solution)/shard_map/all_gather | solution.py:70
  292.3 780.0 %reduce-scatter.5.cloned.1.call-start = ((), (), s32[]{:S(2)}) async-start(), calls=%async_computation.4 | async-start | bytes 8650752 | tf_op jit(solution)/shard_map/reduce_scatter | solution.py:69
  327.1 4.4 copy-start.2
Sparse Core Ops, SparseCore 0:
  11.5 113.3 all-gather.5
  158.7 128.8 reduce-scatter.2
  290.5 36.5 all-gather.7
  329.4 485.1 all-gather.9
  817.5 254.7 reduce-scatter.4
